TPU v7x, 512 devices: a whole 4x8x8 slice. The times are simulated.
512 devices in a mesh: section: 16 (over x_hi, y), dp: 8 (over z), mp: 4 (over x_lo, core).
Axes of the slice: x: 4 (x_hi: 2, x_lo: 2; x = x_hi * 2 + x_lo), y: 8, z: 8, core: 2. Of those that a mesh axis runs over, the one named last changes fastest.
Arguments:
- cotangent: bfloat16 [1024, 4096], P('dp', 'mp'), may hold values from -6 to 6
- saved_inputs: bfloat16 [16, 1024, 4096], P('section', 'dp', 'mp'), may hold values from -6 to 6
- pre_acts: bfloat16 [16, 1024, 4096], P('section', 'dp', 'mp'), may hold values from -8 to 8
- weights: bfloat16 [16, 4096, 4096], P('section', 'mp', 'dp'), may hold values from -0.046875 to 0.046875
- proj_in: bfloat16 [16, 4096, 64], P('section', 'mp'), may hold values from -0.09375 to 0.09375
- proj_out: bfloat16 [16, 4096, 64], P('section', 'mp'), may hold values from -0.09375 to 0.09375
- query_panels: float32 [16, 16, 4096], P('section', 'dp', 'mp'), may hold values from -4 to 4
- partners: int32 [8, 8], replicated, may hold values from 0 to 7, as said below
Outputs:
- train_panels: float32 [16, 32, 4096], P('section', 'dp', 'mp')
- scores: float32 [16, 8, 4], replicated
Inputs may be any that keep to these rules, and one draw needn't show every extreme that they name: The plan has 8 rounds: one round pairs every dp index with itself, and the others are the rounds of one round-robin plan of the 8 indices. The rows of partners hold each of these rounds once, in some order, so partners[r, partners[r, i]] = i.
All inputs are finite; a program needn't handle non-finite values.
Results may differ from a plain program's by a relative error of at most 0.02.
Values may be sent and summed in bfloat16 or wider, within the bound.
No kernel may reach another device: no remote copies, remote signals or barrier semaphores. Data moves between devices by JAX's collectives and lax.ppermute only.
A program may use at most 64 MiB of HBM per device.

v0:
```python
import math
import jax
import jax.numpy as jnp
from jax import lax
from jax.sharding import PartitionSpec as P

LEN = 32


def from_behind(block, axis, distance):
    devices = range(lax.axis_size(axis))
    route = [(i - distance, i) for i in devices if i - distance in devices]
    return lax.ppermute(block, axis, route)


def silu_slope(pre_state):
    sigma = jax.nn.sigmoid(pre_state)
    return sigma * (1.0 + pre_state * (1.0 - sigma))


def score_pair(query_rows, train_rows):
    return jnp.dot(query_rows, train_rows.T, precision=lax.Precision.HIGHEST)


def place_block(score_table, block, row_at, col_at):
    return lax.dynamic_update_slice(
        score_table,
        block[None, None],
        (jnp.asarray(row_at, jnp.int32), jnp.int32(col_at), jnp.int32(0), jnp.int32(0)),
    )


def body(cotangent, saved_inputs, pre_acts, weights, proj_in, proj_out, query_panels, partners):
    section_count = lax.axis_size("section")
    model_count = lax.axis_size("mp")
    data_count = lax.axis_size("dp")
    section_index = lax.axis_index("section")
    model_index = lax.axis_index("mp")
    data_index = lax.axis_index("dp")
    inputs = saved_inputs[0]
    pre_state = pre_acts[0]
    columns = inputs.shape[1]
    length = LEN
    examples = inputs.shape[0] // length
    low_rank = proj_in.shape[2]
    w_rows = lax.all_gather(weights[0], "dp", axis=1, tiled=True)
    step_count = examples + section_count - 1
    top_section = section_count - 1

    def advance(turn, carry):
        outgoing, stored, side_store = carry
        received = from_behind(outgoing, "section", -1)
        example_at = turn - (top_section - section_index)
        active = jnp.logical_and(example_at >= 0, example_at < examples)
        row_start = jnp.clip(example_at, 0, examples - 1) * length
        top_grad = lax.dynamic_slice_in_dim(cotangent, row_start, length, 0)
        delta_piece = jnp.where(section_index == top_section, top_grad, received)
        slopes = silu_slope(
            lax.dynamic_slice_in_dim(pre_state, row_start, length, 0).astype(jnp.float32)
        )
        grad_piece = (delta_piece.astype(jnp.float32) * slopes).astype(jnp.bfloat16)
        grad_full = lax.all_gather(grad_piece, "mp", axis=1, tiled=True)

        def through():
            back_term = lax.dot_general(
                grad_full, w_rows, (((1,), (1,)), ((), ())), preferred_element_type=jnp.float32
            )
            return (delta_piece.astype(jnp.float32) + back_term).astype(jnp.bfloat16)

        def skipped():
            return jnp.zeros_like(delta_piece)

        passed = lax.cond(active, through, skipped)
        previous = lax.dynamic_slice_in_dim(stored, row_start, length, 0)
        stored = lax.dynamic_update_slice_in_dim(
            stored, jnp.where(active, grad_piece, previous), row_start, 0
        )
        return (passed, stored, side_store)

    initial = (
        jnp.zeros((length, columns), jnp.bfloat16),
        jnp.zeros((inputs.shape[0], columns), jnp.bfloat16),
        jnp.zeros((inputs.shape[0], low_rank), jnp.float32),
    )
    final_state = lax.fori_loop(0, step_count, advance, initial)
    stored = final_state[1]
    side_store = final_state[2]
    in_part = jnp.dot(inputs, proj_in[0], preferred_element_type=jnp.float32)
    out_part = jnp.dot(stored, proj_out[0], preferred_element_type=jnp.float32)
    in_side, out_side = (
        lax.psum(in_part.astype(jnp.bfloat16), "mp").astype(jnp.float32),
        lax.psum(out_part.astype(jnp.bfloat16), "mp").astype(jnp.float32),
    )
    piece_rank = low_rank // model_count
    in_rows = lax.dynamic_slice_in_dim(in_side, model_index * piece_rank, piece_rank, 1)
    panels_here = jnp.einsum(
        "etr,etc->erc",
        in_rows.reshape(examples, length, piece_rank),
        out_side.reshape(examples, length, low_rank),
        precision=lax.Precision.HIGHEST,
    ) / math.sqrt(length)
    panels_here = panels_here.reshape(examples, piece_rank * low_rank)
    queries = query_panels[0]
    asked = queries.shape[0]
    rounds = partners.shape[0]
    score_scale = 1.0 / (low_rank * math.sqrt(section_count))
    score_table = jnp.zeros((data_count, rounds, asked, examples), jnp.float32)
    everyone = lax.all_gather(panels_here, "dp", axis=0, tiled=True).reshape(
        data_count, examples, -1
    )
    for round_at in range(rounds):
        partner = partners[round_at, data_index]
        chosen = lax.dynamic_index_in_dim(everyone, partner, 0, keepdims=False)
        score_table = place_block(score_table, score_pair(queries, chosen), data_index, round_at)
    summed = lax.psum(score_table * score_scale, ("section", "dp", "mp"))
    scores = summed.transpose(0, 2, 1, 3).reshape(data_count * asked, rounds, examples)
    return (panels_here[None], scores)


def solution(mesh):
    placed = (
        P("dp", "mp"),
        P("section", "dp", "mp"),
        P("section", "dp", "mp"),
        P("section", "mp", "dp"),
        P("section", "mp", None),
        P("section", "mp", None),
        P("section", "dp", "mp"),
        P(),
    )
    return jax.shard_map(
        body, mesh=mesh, in_specs=placed, out_specs=(P("section", "dp", "mp"), P()), check_vma=False
    )
```

profile of v0, /device:TPU:1, one launch (start us, length us, event | category | flops | bytes accessed | tf_op | source)
XLA Modules:
  0.0 635.7 jit_solution(11931362347134518088)
XLA Ops:
  7.9 1.7 constant_dynamic-slice_fusion.2
  25.3 87.9 %all-gather.4.cloned.1.call-done = bf16[1,1024,4096]{2,1,0:T(8,128)(2,1)} async-done(((bf16[1,1024,512]{2,1,0:T(8,128)(2,1)}), bf16[1,1024,4096]{2,1,0:T(8,128)(2,1)}) %all-gather.4.cloned.1.call-update) | async-done | bytes 8388624 | tf_op jit(solution)/shard_map/all_gather | solution.py:46
  113.8 380.4 %while.17 = (s32[]{:T(128)}, bf16[32,1024]{1,0:T(8,128)(2,1)}, bf16[128,1024]{1,0:T(8,128)(2,1)S(1)}, s32[]{:T(128)}, pred[]{:T(512)}, /*index=5*/bf16[128,1024]...) while((s32[]{:T(128)}, bf16[32,1024]{1,0:T(8,128)(2,1)}, ...), condition=%wide.region_4.5_spmd, body=%wide.region_1.4_spmd.sunk | while | flops 268959744 | bytes 9830719 | solution.py:85
  113.9 1.4 collective-permute-start
  115.3 3.9 collective-permute-done
  120.2 7.4 %all_gather.18 = bf16[32,4096]{1,0:T(8,128)(2,1)S(1)} all-gather(bf16[32,1024]{1,0:T(8,128)(2,1)S(1)} %get-tuple-element.282), channel_id=1, replica_groups=mesh['section'=16,'dp'=8,'mp'=4] {'mp'}, dimensions={1}, use_global_device_ids=true | all-gather | bytes 327680 | tf_op jit(solution)/shard_map/while/body/eval_jaxpr/all_gather | solution.py:62
  128.2 1.3 collective-permute-start
  129.6 4.3 collective-permute-done
  134.8 6.6 %all_gather.18 = bf16[32,4096]{1,0:T(8,128)(2,1)S(1)} all-gather(bf16[32,1024]{1,0:T(8,128)(2,1)S(1)} %get-tuple-element.282), channel_id=1, replica_groups=mesh['section'=16,'dp'=8,'mp'=4] {'mp'}, dimensions={1}, use_global_device_ids=true | all-gather | bytes 327680 | tf_op jit(solution)/shard_map/while/body/eval_jaxpr/all_gather | solution.py:62
  142.1 1.3 collective-permute-start
  143.4 4.3 collective-permute-done
  148.7 6.6 %all_gather.18 = bf16[32,4096]{1,0:T(8,128)(2,1)S(1)} all-gather(bf16[32,1024]{1,0:T(8,128)(2,1)S(1)} %get-tuple-element.282), channel_id=1, replica_groups=mesh['section'=16,'dp'=8,'mp'=4] {'mp'}, dimensions={1}, use_global_device_ids=true | all-gather | bytes 327680 | tf_op jit(solution)/shard_map/while/body/eval_jaxpr/all_gather | solution.py:62
  155.9 1.3 collective-permute-start
  157.2 5.0 collective-permute-done
  163.2 6.4 %all_gather.18 = bf16[32,4096]{1,0:T(8,128)(2,1)S(1)} all-gather(bf16[32,1024]{1,0:T(8,128)(2,1)S(1)} %get-tuple-element.282), channel_id=1, replica_groups=mesh['section'=16,'dp'=8,'mp'=4] {'mp'}, dimensions={1}, use_global_device_ids=true | all-gather | bytes 327680 | tf_op jit(solution)/shard_map/while/body/eval_jaxpr/all_gather | solution.py:62
  170.1 1.3 collective-permute-start
  171.5 5.8 collective-permute-done
  178.2 6.4 %all_gather.18 = bf16[32,4096]{1,0:T(8,128)(2,1)S(1)} all-gather(bf16[32,1024]{1,0:T(8,128)(2,1)S(1)} %get-tuple-element.282), channel_id=1, replica_groups=mesh['section'=16,'dp'=8,'mp'=4] {'mp'}, dimensions={1}, use_global_device_ids=true | all-gather | bytes 327680 | tf_op jit(solution)/shard_map/while/body/eval_jaxpr/all_gather | solution.py:62
  185.2 1.3 collective-permute-start
  186.5 5.8 collective-permute-done
  193.2 6.4 %all_gather.18 = bf16[32,4096]{1,0:T(8,128)(2,1)S(1)} all-gather(bf16[32,1024]{1,0:T(8,128)(2,1)S(1)} %get-tuple-element.282), channel_id=1, replica_groups=mesh['section'=16,'dp'=8,'mp'=4] {'mp'}, dimensions={1}, use_global_device_ids=true | all-gather | bytes 327680 | tf_op jit(solution)/shard_map/while/body/eval_jaxpr/all_gather | solution.py:62
  200.2 1.3 collective-permute-start
  201.5 5.8 collective-permute-done
  208.2 6.4 %all_gather.18 = bf16[32,4096]{1,0:T(8,128)(2,1)S(1)} all-gather(bf16[32,1024]{1,0:T(8,128)(2,1)S(1)} %get-tuple-element.282), channel_id=1, replica_groups=mesh['section'=16,'dp'=8,'mp'=4] {'mp'}, dimensions={1}, use_global_device_ids=true | all-gather | bytes 327680 | tf_op jit(solution)/shard_map/while/body/eval_jaxpr/all_gather | solution.py:62
  215.2 1.3 collective-permute-start
  216.5 5.8 collective-permute-done
  223.2 6.4 %all_gather.18 = bf16[32,4096]{1,0:T(8,128)(2,1)S(1)} all-gather(bf16[32,1024]{1,0:T(8,128)(2,1)S(1)} %get-tuple-element.282), channel_id=1, replica_groups=mesh['section'=16,'dp'=8,'mp'=4] {'mp'}, dimensions={1}, use_global_device_ids=true | all-gather | bytes 327680 | tf_op jit(solution)/shard_map/while/body/eval_jaxpr/all_gather | solution.py:62
  230.2 1.3 collective-permute-start
  231.5 5.8 collective-permute-done
  238.3 6.4 %all_gather.18 = bf16[32,4096]{1,0:T(8,128)(2,1)S(1)} all-gather(bf16[32,1024]{1,0:T(8,128)(2,1)S(1)} %get-tuple-element.282), channel_id=1, replica_groups=mesh['section'=16,'dp'=8,'mp'=4] {'mp'}, dimensions={1}, use_global_device_ids=true | all-gather | bytes 327680 | tf_op jit(solution)/shard_map/while/body/eval_jaxpr/all_gather | solution.py:62
  245.3 1.3 collective-permute-start
  246.6 5.8 collective-permute-done
  253.3 6.4 %all_gather.18 = bf16[32,4096]{1,0:T(8,128)(2,1)S(1)} all-gather(bf16[32,1024]{1,0:T(8,128)(2,1)S(1)} %get-tuple-element.282), channel_id=1, replica_groups=mesh['section'=16,'dp'=8,'mp'=4] {'mp'}, dimensions={1}, use_global_device_ids=true | all-gather | bytes 327680 | tf_op jit(solution)/shard_map/while/body/eval_jaxpr/all_gather | solution.py:62
  260.3 1.3 collective-permute-start
  261.6 8.1 %collective-permute-done = bf16[32,1024]{1,0:T(8,128)(2,1)S(1)} collective-permute-done((bf16[32,1024]{1,0:T(8,128)(2,1)}, bf16[32,1024]{1,0:T(8,128)(2,1)S(1)}, u32[]{:S(2)}, u32[]{:S(2)}) %collective-permute-start) | collective-permute-done | bytes 65568 | tf_op jit(solution)/shard_map/while/body/eval_jaxpr/ppermute | solution.py:13
  270.6 6.4 %all_gather.18 = bf16[32,4096]{1,0:T(8,128)(2,1)S(1)} all-gather(bf16[32,1024]{1,0:T(8,128)(2,1)S(1)} %get-tuple-element.282), channel_id=1, replica_groups=mesh['section'=16,'dp'=8,'mp'=4] {'mp'}, dimensions={1}, use_global_device_ids=true | all-gather | bytes 327680 | tf_op jit(solution)/shard_map/while/body/eval_jaxpr/all_gather | solution.py:62
  277.6 1.3 collective-permute-start
  278.9 8.2 %collective-permute-done = bf16[32,1024]{1,0:T(8,128)(2,1)S(1)} collective-permute-done((bf16[32,1024]{1,0:T(8,128)(2,1)}, bf16[32,1024]{1,0:T(8,128)(2,1)S(1)}, u32[]{:S(2)}, u32[]{:S(2)}) %collective-permute-start) | collective-permute-done | bytes 65568 | tf_op jit(solution)/shard_map/while/body/eval_jaxpr/ppermute | solution.py:13
  288.0 6.4 %all_gather.18 = bf16[32,4096]{1,0:T(8,128)(2,1)S(1)} all-gather(bf16[32,1024]{1,0:T(8,128)(2,1)S(1)} %get-tuple-element.282), channel_id=1, replica_groups=mesh['section'=16,'dp'=8,'mp'=4] {'mp'}, dimensions={1}, use_global_device_ids=true | all-gather | bytes 327680 | tf_op jit(solution)/shard_map/while/body/eval_jaxpr/all_gather | solution.py:62
  296.3 8.2 %collective-permute-done = bf16[32,1024]{1,0:T(8,128)(2,1)S(1)} collective-permute-done((bf16[32,1024]{1,0:T(8,128)(2,1)}, bf16[32,1024]{1,0:T(8,128)(2,1)S(1)}, u32[]{:S(2)}, u32[]{:S(2)}) %collective-permute-start) | collective-permute-done | bytes 65568 | tf_op jit(solution)/shard_map/while/body/eval_jaxpr/ppermute | solution.py:13
  305.5 6.4 %all_gather.18 = bf16[32,4096]{1,0:T(8,128)(2,1)S(1)} all-gather(bf16[32,1024]{1,0:T(8,128)(2,1)S(1)} %get-tuple-element.282), channel_id=1, replica_groups=mesh['section'=16,'dp'=8,'mp'=4] {'mp'}, dimensions={1}, use_global_device_ids=true | all-gather | bytes 327680 | tf_op jit(solution)/shard_map/while/body/eval_jaxpr/all_gather | solution.py:62
  313.8 8.2 %collective-permute-done = bf16[32,1024]{1,0:T(8,128)(2,1)S(1)} collective-permute-done((bf16[32,1024]{1,0:T(8,128)(2,1)}, bf16[32,1024]{1,0:T(8,128)(2,1)S(1)}, u32[]{:S(2)}, u32[]{:S(2)}) %collective-permute-start) | collective-permute-done | bytes 65568 | tf_op jit(solution)/shard_map/while/body/eval_jaxpr/ppermute | solution.py:13
  322.9 6.4 %all_gather.18 = bf16[32,4096]{1,0:T(8,128)(2,1)S(1)} all-gather(bf16[32,1024]{1,0:T(8,128)(2,1)S(1)} %get-tuple-element.282), channel_id=1, replica_groups=mesh['section'=16,'dp'=8,'mp'=4] {'mp'}, dimensions={1}, use_global_device_ids=true | all-gather | bytes 327680 | tf_op jit(solution)/shard_map/while/body/eval_jaxpr/all_gather | solution.py:62
  331.2 8.2 %collective-permute-done = bf16[32,1024]{1,0:T(8,128)(2,1)S(1)} collective-permute-done((bf16[32,1024]{1,0:T(8,128)(2,1)}, bf16[32,1024]{1,0:T(8,128)(2,1)S(1)}, u32[]{:S(2)}, u32[]{:S(2)}) %collective-permute-start) | collective-permute-done | bytes 65568 | tf_op jit(solution)/shard_map/while/body/eval_jaxpr/ppermute | solution.py:13
  340.3 6.4 %all_gather.18 = bf16[32,4096]{1,0:T(8,128)(2,1)S(1)} all-gather(bf16[32,1024]{1,0:T(8,128)(2,1)S(1)} %get-tuple-element.282), channel_id=1, replica_groups=mesh['section'=16,'dp'=8,'mp'=4] {'mp'}, dimensions={1}, use_global_device_ids=true | all-gather | bytes 327680 | tf_op jit(solution)/shard_map/while/body/eval_jaxpr/all_gather | solution.py:62
  348.6 61.6 %collective-permute-done = bf16[32,1024]{1,0:T(8,128)(2,1)S(1)} collective-permute-done((bf16[32,1024]{1,0:T(8,128)(2,1)}, bf16[32,1024]{1,0:T(8,128)(2,1)S(1)}, u32[]{:S(2)}, u32[]{:S(2)}) %collective-permute-start) | collective-permute-done | bytes 65568 | tf_op jit(solution)/shard_map/while/body/eval_jaxpr/ppermute | solution.py:13
  411.2 6.3 all_gather.18
  417.5 6.6 %conditional.2 = (bf16[32,1024]{1,0:T(8,128)(2,1)}) conditional(s32[]{:T(128)} %convert_element_type.80, () %tuple.60, (bf16[32,1024]{1,0:T(8,128)(2,1)S(1)}, bf16[32,4096]{1,0:T(8,128)(2,1)S(1)}, bf16[1024,4096]{1,0:T(8,128)(2,1)}) %tuple.61), branch_computations={%region_2.2_spmd, %region_3.3_spmd} | conditional | flops 268533760 | bytes 8781832 | solution.py:73
  417.5 6.6 %fusion = bf16[32,1024]{1,0:T(8,128)(2,1)} fusion(bf16[32,4096]{1,0:T(8,128)(2,1)S(1)} %get-tuple-element.181, bf16[1024,4096]{1,0:T(8,128)(2,1)} %get-tuple-element.182, bf16[32,1024]{1,0:T(8,128)(2,1)S(1)} %get-tuple-element.180), kind=kOutput, calls=%fused_computation.1 | convolution fusion | flops 268533760 | bytes 8781824 | tf_op jit(solution)/shard_map/while/body/eval_jaxpr/cond/branch_1_fun/dot_general | solution.py:65
  425.4 8.2 %collective-permute-done = bf16[32,1024]{1,0:T(8,128)(2,1)S(1)} collective-permute-done((bf16[32,1024]{1,0:T(8,128)(2,1)}, bf16[32,1024]{1,0:T(8,128)(2,1)S(1)}, u32[]{:S(2)}, u32[]{:S(2)}) %collective-permute-start) | collective-permute-done | bytes 65568 | tf_op jit(solution)/shard_map/while/body/eval_jaxpr/ppermute | solution.py:13
  434.6 6.3 all_gather.18
  440.8 6.6 %conditional.2 = (bf16[32,1024]{1,0:T(8,128)(2,1)}) conditional(s32[]{:T(128)} %convert_element_type.80, () %tuple.60, (bf16[32,1024]{1,0:T(8,128)(2,1)S(1)}, bf16[32,4096]{1,0:T(8,128)(2,1)S(1)}, bf16[1024,4096]{1,0:T(8,128)(2,1)}) %tuple.61), branch_computations={%region_2.2_spmd, %region_3.3_spmd} | conditional | flops 268533760 | bytes 8781832 | solution.py:73
  440.8 6.6 %fusion = bf16[32,1024]{1,0:T(8,128)(2,1)} fusion(bf16[32,4096]{1,0:T(8,128)(2,1)S(1)} %get-tuple-element.181, bf16[1024,4096]{1,0:T(8,128)(2,1)} %get-tuple-element.182, bf16[32,1024]{1,0:T(8,128)(2,1)S(1)} %get-tuple-element.180), kind=kOutput, calls=%fused_computation.1 | convolution fusion | flops 268533760 | bytes 8781824 | tf_op jit(solution)/shard_map/while/body/eval_jaxpr/cond/branch_1_fun/dot_general | solution.py:65
  448.7 8.3 %collective-permute-done = bf16[32,1024]{1,0:T(8,128)(2,1)S(1)} collective-permute-done((bf16[32,1024]{1,0:T(8,128)(2,1)}, bf16[32,1024]{1,0:T(8,128)(2,1)S(1)}, u32[]{:S(2)}, u32[]{:S(2)}) %collective-permute-start) | collective-permute-done | bytes 65568 | tf_op jit(solution)/shard_map/while/body/eval_jaxpr/ppermute | solution.py:13
  458.0 6.3 all_gather.18
  464.3 6.6 %conditional.2 = (bf16[32,1024]{1,0:T(8,128)(2,1)}) conditional(s32[]{:T(128)} %convert_element_type.80, () %tuple.60, (bf16[32,1024]{1,0:T(8,128)(2,1)S(1)}, bf16[32,4096]{1,0:T(8,128)(2,1)S(1)}, bf16[1024,4096]{1,0:T(8,128)(2,1)}) %tuple.61), branch_computations={%region_2.2_spmd, %region_3.3_spmd} | conditional | flops 268533760 | bytes 8781832 | solution.py:73
  464.3 6.6 %fusion = bf16[32,1024]{1,0:T(8,128)(2,1)} fusion(bf16[32,4096]{1,0:T(8,128)(2,1)S(1)} %get-tuple-element.181, bf16[1024,4096]{1,0:T(8,128)(2,1)} %get-tuple-element.182, bf16[32,1024]{1,0:T(8,128)(2,1)S(1)} %get-tuple-element.180), kind=kOutput, calls=%fused_computation.1 | convolution fusion | flops 268533760 | bytes 8781824 | tf_op jit(solution)/shard_map/while/body/eval_jaxpr/cond/branch_1_fun/dot_general | solution.py:65
  472.2 8.2 %collective-permute-done = bf16[32,1024]{1,0:T(8,128)(2,1)S(1)} collective-permute-done((bf16[32,1024]{1,0:T(8,128)(2,1)}, bf16[32,1024]{1,0:T(8,128)(2,1)S(1)}, u32[]{:S(2)}, u32[]{:S(2)}) %collective-permute-start) | collective-permute-done | bytes 65568 | tf_op jit(solution)/shard_map/while/body/eval_jaxpr/ppermute | solution.py:13
  481.4 6.3 all_gather.18
  487.7 6.6 %conditional.2 = (bf16[32,1024]{1,0:T(8,128)(2,1)}) conditional(s32[]{:T(128)} %convert_element_type.80, () %tuple.60, (bf16[32,1024]{1,0:T(8,128)(2,1)S(1)}, bf16[32,4096]{1,0:T(8,128)(2,1)S(1)}, bf16[1024,4096]{1,0:T(8,128)(2,1)}) %tuple.61), branch_computations={%region_2.2_spmd, %region_3.3_spmd} | conditional | flops 268533760 | bytes 8781832 | solution.py:73
  487.7 6.6 %fusion = bf16[32,1024]{1,0:T(8,128)(2,1)} fusion(bf16[32,4096]{1,0:T(8,128)(2,1)S(1)} %get-tuple-element.181, bf16[1024,4096]{1,0:T(8,128)(2,1)} %get-tuple-element.182, bf16[32,1024]{1,0:T(8,128)(2,1)S(1)} %get-tuple-element.180), kind=kOutput, calls=%fused_computation.1 | convolution fusion | flops 268533760 | bytes 8781824 | tf_op jit(solution)/shard_map/while/body/eval_jaxpr/cond/branch_1_fun/dot_general | solution.py:65
  494.6 10.8 %all-reduce = (bf16[4,32,64]{2,1,0:T(8,128)(2,1)S(1)}, bf16[128,64]{0,1:T(8,128)(2,1)S(1)}) all-reduce(bf16[4,32,64]{2,1,0:T(8,128)(2,1)S(1)} %bitcast.104, bf16[128,64]{0,1:T(8,128)(2,1)S(1)} %convolution_convert_fusion.1), channel_id=1, replica_groups=mesh['section'=16,'dp'=8,'mp'=4] {'mp'}, use_global_device_ids=true, to_apply=%region_5.6 | all-reduce | flops 16384 | bytes 65536 | tf_op jit(solution)/shard_map/psum | solution.py:92
  505.7 18.5 %all-gather.1 = f32[8,4,1024]{2,1,0:T(4,128)S(1)} all-gather(f32[1,4,1024]{2,1,0:T(4,128)S(1)} %broadcast_in_dim_reshape.3), channel_id=1, replica_groups=mesh['section'=16,'dp'=8,'mp'=4] {'dp'}, dimensions={0}, use_global_device_ids=true | all-gather | bytes 147456 | tf_op jit(solution)/shard_map/all_gather | solution.py:108
  529.0 99.2 %psum.23 = f32[16,8,4]{1,0,2:T(8,128)S(1)} all-reduce(f32[16,8,4]{1,0,2:T(8,128)S(1)} %bitcast.105), channel_id=1, replica_groups=mesh['section'=16,'dp'=8,'mp'=4] {'section','dp','mp'}, use_global_device_ids=true, to_apply=%region_6.7 | all-reduce | flops 512 | bytes 4096 | tf_op jit(solution)/shard_map/psum | solution.py:115
  (102 shorter events, 54.5 us)
Async XLA Ops:
  7.2 17.0 %copy-start = (bf16[1,128,1024]{2,1,0:T(8,128)(2,1)S(1)}, bf16[1,128,1024]{2,1,0:T(8,128)(2,1)}, u32[]{:S(2)}) copy-start(bf16[1,128,1024]{2,1,0:T(8,128)(2,1)} %param.13) | copy-start | bytes 786436
  7.2 106.0 %all-gather.4.cloned.1.call-start = ((), (), s32[]{:S(2)}) async-start(), calls=%async_computation | async-start | bytes 9437184 | tf_op jit(solution)/shard_map/all_gather | solution.py:46
  113.8 380.5 %copy-start.2 = (bf16[1,1024,64]{1,2,0:T(8,128)(2,1)S(1)}, bf16[1,1024,64]{1,2,0:T(8,128)(2,1)}, u32[]{:S(2)}) copy-start(bf16[1,1024,64]{1,2,0:T(8,128)(2,1)} %param.17) | copy-start | bytes 393220
  113.8 410.4 %copy-start.1 = (f32[1,2,1024]{2,1,0:T(2,128)S(1)}, f32[1,2,1024]{2,1,0:T(2,128)}, u32[]{:S(2)}) copy-start(f32[1,2,1024]{2,1,0:T(2,128)} %param.18) | copy-start | bytes 24580
  113.9 5.4 collective-permute-start
  128.2 5.6 collective-permute-start
  142.1 5.6 collective-permute-start
  155.9 6.3 collective-permute-start
  170.1 7.1 %collective-permute-start = (bf16[32,1024]{1,0:T(8,128)(2,1)}, bf16[32,1024]{1,0:T(8,128)(2,1)S(1)}, u32[]{:S(2)}, u32[]{:S(2)}) collective-permute-start(bf16[32,1024]{1,0:T(8,128)(2,1)} %get-tuple-element.299), channel_id=1, source_target_pairs={{32,0},{64,32},{96,64},{128,96},{160,128},{192,160},{224,192},{256... | collective-permute-start | bytes 196616 | tf_op jit(solution)/shard_map/while/body/eval_jaxpr/ppermute | solution.py:13
  185.2 7.1 %collective-permute-start = (bf16[32,1024]{1,0:T(8,128)(2,1)}, bf16[32,1024]{1,0:T(8,128)(2,1)S(1)}, u32[]{:S(2)}, u32[]{:S(2)}) collective-permute-start(bf16[32,1024]{1,0:T(8,128)(2,1)} %get-tuple-element.299), channel_id=1, source_target_pairs={{32,0},{64,32},{96,64},{128,96},{160,128},{192,160},{224,192},{256... | collective-permute-start | bytes 196616 | tf_op jit(solution)/shard_map/while/body/eval_jaxpr/ppermute | solution.py:13
  200.2 7.1 %collective-permute-start = (bf16[32,1024]{1,0:T(8,128)(2,1)}, bf16[32,1024]{1,0:T(8,128)(2,1)S(1)}, u32[]{:S(2)}, u32[]{:S(2)}) collective-permute-start(bf16[32,1024]{1,0:T(8,128)(2,1)} %get-tuple-element.299), channel_id=1, source_target_pairs={{32,0},{64,32},{96,64},{128,96},{160,128},{192,160},{224,192},{256... | collective-permute-start | bytes 196616 | tf_op jit(solution)/shard_map/while/body/eval_jaxpr/ppermute | solution.py:13
  215.2 7.1 %collective-permute-start = (bf16[32,1024]{1,0:T(8,128)(2,1)}, bf16[32,1024]{1,0:T(8,128)(2,1)S(1)}, u32[]{:S(2)}, u32[]{:S(2)}) collective-permute-start(bf16[32,1024]{1,0:T(8,128)(2,1)} %get-tuple-element.299), channel_id=1, source_target_pairs={{32,0},{64,32},{96,64},{128,96},{160,128},{192,160},{224,192},{256... | collective-permute-start | bytes 196616 | tf_op jit(solution)/shard_map/while/body/eval_jaxpr/ppermute | solution.py:13
  230.2 7.1 %collective-permute-start = (bf16[32,1024]{1,0:T(8,128)(2,1)}, bf16[32,1024]{1,0:T(8,128)(2,1)S(1)}, u32[]{:S(2)}, u32[]{:S(2)}) collective-permute-start(bf16[32,1024]{1,0:T(8,128)(2,1)} %get-tuple-element.299), channel_id=1, source_target_pairs={{32,0},{64,32},{96,64},{128,96},{160,128},{192,160},{224,192},{256... | collective-permute-start | bytes 196616 | tf_op jit(solution)/shard_map/while/body/eval_jaxpr/ppermute | solution.py:13
  245.3 7.1 %collective-permute-start = (bf16[32,1024]{1,0:T(8,128)(2,1)}, bf16[32,1024]{1,0:T(8,128)(2,1)S(1)}, u32[]{:S(2)}, u32[]{:S(2)}) collective-permute-start(bf16[32,1024]{1,0:T(8,128)(2,1)} %get-tuple-element.299), channel_id=1, source_target_pairs={{32,0},{64,32},{96,64},{128,96},{160,128},{192,160},{224,192},{256... | collective-permute-start | bytes 196616 | tf_op jit(solution)/shard_map/while/body/eval_jaxpr/ppermute | solution.py:13
  260.3 9.4 %collective-permute-start = (bf16[32,1024]{1,0:T(8,128)(2,1)}, bf16[32,1024]{1,0:T(8,128)(2,1)S(1)}, u32[]{:S(2)}, u32[]{:S(2)}) collective-permute-start(bf16[32,1024]{1,0:T(8,128)(2,1)} %get-tuple-element.299), channel_id=1, source_target_pairs={{32,0},{64,32},{96,64},{128,96},{160,128},{192,160},{224,192},{256... | collective-permute-start | bytes 196616 | tf_op jit(solution)/shard_map/while/body/eval_jaxpr/ppermute | solution.py:13
  277.6 9.5 %collective-permute-start = (bf16[32,1024]{1,0:T(8,128)(2,1)}, bf16[32,1024]{1,0:T(8,128)(2,1)S(1)}, u32[]{:S(2)}, u32[]{:S(2)}) collective-permute-start(bf16[32,1024]{1,0:T(8,128)(2,1)} %get-tuple-element.299), channel_id=1, source_target_pairs={{32,0},{64,32},{96,64},{128,96},{160,128},{192,160},{224,192},{256... | collective-permute-start | bytes 196616 | tf_op jit(solution)/shard_map/while/body/eval_jaxpr/ppermute | solution.py:13
  295.0 9.5 %collective-permute-start = (bf16[32,1024]{1,0:T(8,128)(2,1)}, bf16[32,1024]{1,0:T(8,128)(2,1)S(1)}, u32[]{:S(2)}, u32[]{:S(2)}) collective-permute-start(bf16[32,1024]{1,0:T(8,128)(2,1)} %get-tuple-element.299), channel_id=1, source_target_pairs={{32,0},{64,32},{96,64},{128,96},{160,128},{192,160},{224,192},{256... | collective-permute-start | bytes 196616 | tf_op jit(solution)/shard_map/while/body/eval_jaxpr/ppermute | solution.py:13
  312.4 9.5 %collective-permute-start = (bf16[32,1024]{1,0:T(8,128)(2,1)}, bf16[32,1024]{1,0:T(8,128)(2,1)S(1)}, u32[]{:S(2)}, u32[]{:S(2)}) collective-permute-start(bf16[32,1024]{1,0:T(8,128)(2,1)} %get-tuple-element.299), channel_id=1, source_target_pairs={{32,0},{64,32},{96,64},{128,96},{160,128},{192,160},{224,192},{256... | collective-permute-start | bytes 196616 | tf_op jit(solution)/shard_map/while/body/eval_jaxpr/ppermute | solution.py:13
  329.9 9.5 %collective-permute-start = (bf16[32,1024]{1,0:T(8,128)(2,1)}, bf16[32,1024]{1,0:T(8,128)(2,1)S(1)}, u32[]{:S(2)}, u32[]{:S(2)}) collective-permute-start(bf16[32,1024]{1,0:T(8,128)(2,1)} %get-tuple-element.299), channel_id=1, source_target_pairs={{32,0},{64,32},{96,64},{128,96},{160,128},{192,160},{224,192},{256... | collective-permute-start | bytes 196616 | tf_op jit(solution)/shard_map/while/body/eval_jaxpr/ppermute | solution.py:13
  347.3 62.9 %collective-permute-start = (bf16[32,1024]{1,0:T(8,128)(2,1)}, bf16[32,1024]{1,0:T(8,128)(2,1)S(1)}, u32[]{:S(2)}, u32[]{:S(2)}) collective-permute-start(bf16[32,1024]{1,0:T(8,128)(2,1)} %get-tuple-element.299), channel_id=1, source_target_pairs={{32,0},{64,32},{96,64},{128,96},{160,128},{192,160},{224,192},{256... | collective-permute-start | bytes 196616 | tf_op jit(solution)/shard_map/while/body/eval_jaxpr/ppermute | solution.py:13
  424.0 9.6 %collective-permute-start = (bf16[32,1024]{1,0:T(8,128)(2,1)}, bf16[32,1024]{1,0:T(8,128)(2,1)S(1)}, u32[]{:S(2)}, u32[]{:S(2)}) collective-permute-start(bf16[32,1024]{1,0:T(8,128)(2,1)} %get-tuple-element.299), channel_id=1, source_target_pairs={{32,0},{64,32},{96,64},{128,96},{160,128},{192,160},{224,192},{256... | collective-permute-start | bytes 196616 | tf_op jit(solution)/shard_map/while/body/eval_jaxpr/ppermute | solution.py:13
  447.4 9.6 %collective-permute-start = (bf16[32,1024]{1,0:T(8,128)(2,1)}, bf16[32,1024]{1,0:T(8,128)(2,1)S(1)}, u32[]{:S(2)}, u32[]{:S(2)}) collective-permute-start(bf16[32,1024]{1,0:T(8,128)(2,1)} %get-tuple-element.299), channel_id=1, source_target_pairs={{32,0},{64,32},{96,64},{128,96},{160,128},{192,160},{224,192},{256... | collective-permute-start | bytes 196616 | tf_op jit(solution)/shard_map/while/body/eval_jaxpr/ppermute | solution.py:13
  470.9 9.6 %collective-permute-start = (bf16[32,1024]{1,0:T(8,128)(2,1)}, bf16[32,1024]{1,0:T(8,128)(2,1)S(1)}, u32[]{:S(2)}, u32[]{:S(2)}) collective-permute-start(bf16[32,1024]{1,0:T(8,128)(2,1)} %get-tuple-element.299), channel_id=1, source_target_pairs={{32,0},{64,32},{96,64},{128,96},{160,128},{192,160},{224,192},{256... | collective-permute-start | bytes 196616 | tf_op jit(solution)/shard_map/while/body/eval_jaxpr/ppermute | solution.py:13
  505.7 123.2 %copy-start.3 = (f32[1,4,1024]{2,1,0:T(4,128)}, f32[1,4,1024]{2,1,0:T(4,128)S(1)}, u32[]{:S(2)}) copy-start(f32[1,4,1024]{2,1,0:T(4,128)S(1)} %broadcast_in_dim_reshape.3) | copy-start | bytes 49156
Sparse Core Ops, SparseCore 0:
  10.1 103.0 all-gather.3
where the time goes:
time: 638 us; the launch traced here: 636 us
  waiting for transfers between devices  268 us (42%)
  blocking collectives  251 us (39%)
  matrix products  29.3 us (5%)
  between operations  28.8 us (5%)
  starting transfers between devices  24.5 us (4%)
  other arithmetic  18.2 us (3%)
  local copies, waits for them, and re-layouts  15.9 us (2%)
    ppermute x19, waiting for transfers between devices, from_behind(): return lax.ppermute(block, axis, route)  179 us
    all_gather x19, blocking collectives, advance(): grad_full = lax.all_gather(grad_piece, 'mp', axis=1, tiled=True)  122 us
    psum x1, blocking collectives, body(): summed = lax.psum(score_table * score_scale, ('section', 'dp', 'mp'))  99.2 us
    all_gather x1, waiting for transfers between devices, body(): w_rows = lax.all_gather(weights[0], 'dp', axis=1, tiled=True)  87.9 us
    dot_general x4, matrix products, through(): lax.dot_general(grad_full, w_rows, (((1,), (1,)), ((), ())), preferred_el...  26.4 us
    ppermute x19, starting transfers between devices, from_behind(): return lax.ppermute(block, axis, route)  24.5 us
    all_gather x1, blocking collectives, body(): lax.all_gather(panels_here, 'dp', axis=0, tiled=True)  18.5 us
    dynamic_update_slice x19, other arithmetic, advance(): lax.dynamic_update_slice_in_dim(stored, jnp.where(active, grad_piece, pre...  18.2 us
  transfers between devices with their start and end apart: 20, of which 20 were waited for; matrix products, arithmetic and copies ran while one was open for 0% of the time, Pallas kernels for 0%

commit v1 on v0

--- a/solution.py
+++ b/solution.py
@@ -1,3 +1,4 @@
+import functools
 import math
 import jax
 import jax.numpy as jnp
@@ -5,6 +6,15 @@
 from jax.sharding import PartitionSpec as P
 
 LEN = 32
+
+
+def supply_rings(xin, dim_at):
+    newest = jnp.stack([xin for _ in range(jax.lax.axis_size("dp"))], 0)
+    now = jax.lax.all_to_all(newest, axis_name="dp", split_axis=0, concat_axis=0)
+    return jnp.concatenate(now, dim_at)
+
+
+answer_counts = functools.partial(supply_rings, dim_at=1)
 
 
 def from_behind(block, axis, distance):
@@ -43,7 +53,7 @@
     length = LEN
     examples = inputs.shape[0] // length
     low_rank = proj_in.shape[2]
-    w_rows = lax.all_gather(weights[0], "dp", axis=1, tiled=True)
+    w_rows = answer_counts(weights[0])
     step_count = examples + section_count - 1
     top_section = section_count - 1
 

time: 638 us -> 744 us (1.17)
  waiting for transfers between devices: 268 us -> 351 us
  local copies, waits for them, and re-layouts: 15.9 us -> 42.8 us
  between operations: 28.8 us -> 15.8 us
  starting transfers between devices: 24.5 us -> 35.4 us
    all_to_all x0 -> x1, waiting for transfers between devices: none -> 171 us  [supply_rings(): jax.lax.all_to_all(newest, axis_name='dp', split_axis=0, concat_axis=0)]
    all_gather x1 -> x0, waiting for transfers between devices: 87.9 us -> none  [body(): w_rows = lax.all_gather(weights[0], 'dp', axis=1, tiled=True)]
    all_to_all x0 -> x1, local copies, waits for them, and re-layouts: none -> 11.4 us  [supply_rings(): jax.lax.all_to_all(newest, axis_name='dp', split_axis=0, concat_axis=0)]
    while x0 -> x1, local copies, waits for them, and re-layouts: none -> 11.3 us  [body(): final_state = lax.fori_loop(0, step_count, advance, initial)]
    all_to_all x0 -> x1, starting transfers between devices: none -> 11 us  [supply_rings(): jax.lax.all_to_all(newest, axis_name='dp', split_axis=0, concat_axis=0)]
    another operation x16 -> x17, local copies, waits for them, and re-layouts: 10.1 us -> 15.2 us
where the time goes in v1:
time: 744 us; the launch traced here: 742 us
  waiting for transfers between devices  351 us (47%)
  blocking collectives  250 us (34%)
  local copies, waits for them, and re-layouts  42.8 us (6%)
  starting transfers between devices  35.4 us (5%)
  matrix products  28.3 us (4%)
  other arithmetic  18.2 us (2%)
  between operations  15.8 us (2%)
    ppermute x19, waiting for transfers between devices, from_behind(): return lax.ppermute(block, axis, route)  180 us
    all_to_all x1, waiting for transfers between devices, supply_rings(): jax.lax.all_to_all(newest, axis_name='dp', split_axis=0, concat_axis=0)  171 us
    all_gather x19, blocking collectives, advance(): grad_full = lax.all_gather(grad_piece, 'mp', axis=1, tiled=True)  122 us
    psum x1, blocking collectives, body(): summed = lax.psum(score_table * score_scale, ('section', 'dp', 'mp'))  98.5 us
    dot_general x4, matrix products, through(): lax.dot_general(grad_full, w_rows, (((1,), (1,)), ((), ())), preferred_el...  26.3 us
    ppermute x19, starting transfers between devices, from_behind(): return lax.ppermute(block, axis, route)  24.5 us
    all_gather x1, blocking collectives, body(): lax.all_gather(panels_here, 'dp', axis=0, tiled=True)  18.4 us
    dynamic_update_slice x19, other arithmetic, advance(): lax.dynamic_update_slice_in_dim(stored, jnp.where(active, grad_piece, pre...  18.2 us
  transfers between devices with their start and end apart: 20, of which 20 were waited for; matrix products, arithmetic and copies ran while one was open for 0% of the time, Pallas kernels for 0%

profile of v1, /device:TPU:1, one launch (start us, length us, event | category | flops | bytes accessed | tf_op | source)
XLA Modules:
  0.0 741.7 jit_solution(6881397531740330886)
XLA Ops:
  0.6 5.2 stack.3
  5.9 11.0 %all-to-all-start = ((bf16[8,1024,512]{2,1,0:T(8,128)(2,1)}), bf16[8,1024,512]{2,1,0:T(8,128)(2,1)}, u32[]{:S(2)}, u32[]{:S(2)}) async-start(bf16[8,1024,512]{2,1,0:T(8,128)(2,1)} %stack.3), calls=%async_computation | async-start | bytes 16777216 | tf_op jit(solution)/shard_map/all_to_all | solution.py:13
  32.8 171.0 %all-to-all-done = bf16[8,1024,512]{2,1,0:T(8,128)(2,1)} async-done(((bf16[8,1024,512]{2,1,0:T(8,128)(2,1)}), bf16[8,1024,512]{2,1,0:T(8,128)(2,1)}, u32[]{:S(2)}, u32[]{:S(2)}) %all-to-all-start) | async-done | bytes 8388640 | tf_op jit(solution)/shard_map/all_to_all | solution.py:13
  203.8 11.4 %copy.41 = bf16[8,1024,512]{1,2,0:T(8,128)(2,1)} copy(bf16[8,1024,512]{2,1,0:T(8,128)(2,1)} %all-to-all-done) | data formatting | bytes 16777216 | tf_op jit(solution)/shard_map/all_to_all | solution.py:13
  215.2 11.3 %copy.42 = bf16[1024,4096]{1,0:T(8,128)(2,1)} copy(bf16[1024,4096]{0,1:T(8,128)(2,1)} %bitcast.105) | data formatting | bytes 16777216 | tf_op jit(solution)/shard_map/while | solution.py:95
  227.1 380.7 %while.17 = (s32[]{:T(128)}, bf16[32,1024]{1,0:T(8,128)(2,1)}, bf16[128,1024]{1,0:T(8,128)(2,1)S(1)}, s32[]{:T(128)}, pred[]{:T(512)}, /*index=5*/bf16[128,1024]...) while((s32[]{:T(128)}, bf16[32,1024]{1,0:T(8,128)(2,1)}, ...), condition=%wide.region_4.5_spmd, body=%wide.region_1.4_spmd.sunk | while | flops 268959744 | bytes 9830719 | solution.py:95
  227.1 1.4 collective-permute-start
  228.6 3.9 collective-permute-done
  233.4 7.3 all_gather.14
  241.3 1.3 collective-permute-start
  242.6 4.3 collective-permute-done
  247.9 6.6 all_gather.14
  255.1 1.3 collective-permute-start
  256.4 4.3 collective-permute-done
  261.7 6.6 all_gather.14
  268.9 1.3 collective-permute-start
  270.2 5.3 collective-permute-done
  276.5 6.4 all_gather.14
  283.5 1.3 collective-permute-start
  284.8 5.8 collective-permute-done
  291.5 6.4 all_gather.14
  298.5 1.3 collective-permute-start
  299.8 5.8 collective-permute-done
  306.5 6.4 all_gather.14
  313.5 1.3 collective-permute-start
  314.8 5.8 collective-permute-done
  321.5 6.4 all_gather.14
  328.5 1.3 collective-permute-start
  329.8 5.8 collective-permute-done
  336.6 6.4 all_gather.14
  343.6 1.3 collective-permute-start
  344.9 5.8 collective-permute-done
  351.6 6.4 all_gather.14
  359.9 6.0 collective-permute-done
  366.9 6.4 all_gather.14
  375.1 8.2 %collective-permute-done = bf16[32,1024]{1,0:T(8,128)(2,1)S(1)} collective-permute-done((bf16[32,1024]{1,0:T(8,128)(2,1)}, bf16[32,1024]{1,0:T(8,128)(2,1)S(1)}, u32[]{:S(2)}, u32[]{:S(2)}) %collective-permute-start) | collective-permute-done | bytes 65568 | tf_op jit(solution)/shard_map/while/body/eval_jaxpr/ppermute | solution.py:23
  384.3 6.4 all_gather.14
  392.6 8.2 %collective-permute-done = bf16[32,1024]{1,0:T(8,128)(2,1)S(1)} collective-permute-done((bf16[32,1024]{1,0:T(8,128)(2,1)}, bf16[32,1024]{1,0:T(8,128)(2,1)S(1)}, u32[]{:S(2)}, u32[]{:S(2)}) %collective-permute-start) | collective-permute-done | bytes 65568 | tf_op jit(solution)/shard_map/while/body/eval_jaxpr/ppermute | solution.py:23
  401.7 6.4 all_gather.14
  410.0 8.2 %collective-permute-done = bf16[32,1024]{1,0:T(8,128)(2,1)S(1)} collective-permute-done((bf16[32,1024]{1,0:T(8,128)(2,1)}, bf16[32,1024]{1,0:T(8,128)(2,1)S(1)}, u32[]{:S(2)}, u32[]{:S(2)}) %collective-permute-start) | collective-permute-done | bytes 65568 | tf_op jit(solution)/shard_map/while/body/eval_jaxpr/ppermute | solution.py:23
  419.1 6.4 all_gather.14
  427.4 8.2 %collective-permute-done = bf16[32,1024]{1,0:T(8,128)(2,1)S(1)} collective-permute-done((bf16[32,1024]{1,0:T(8,128)(2,1)}, bf16[32,1024]{1,0:T(8,128)(2,1)S(1)}, u32[]{:S(2)}, u32[]{:S(2)}) %collective-permute-start) | collective-permute-done | bytes 65568 | tf_op jit(solution)/shard_map/while/body/eval_jaxpr/ppermute | solution.py:23
  436.5 6.4 all_gather.14
  444.8 8.2 %collective-permute-done = bf16[32,1024]{1,0:T(8,128)(2,1)S(1)} collective-permute-done((bf16[32,1024]{1,0:T(8,128)(2,1)}, bf16[32,1024]{1,0:T(8,128)(2,1)S(1)}, u32[]{:S(2)}, u32[]{:S(2)}) %collective-permute-start) | collective-permute-done | bytes 65568 | tf_op jit(solution)/shard_map/while/body/eval_jaxpr/ppermute | solution.py:23
  454.0 6.4 all_gather.14
  462.2 61.6 %collective-permute-done = bf16[32,1024]{1,0:T(8,128)(2,1)S(1)} collective-permute-done((bf16[32,1024]{1,0:T(8,128)(2,1)}, bf16[32,1024]{1,0:T(8,128)(2,1)S(1)}, u32[]{:S(2)}, u32[]{:S(2)}) %collective-permute-start) | collective-permute-done | bytes 65568 | tf_op jit(solution)/shard_map/while/body/eval_jaxpr/ppermute | solution.py:23
  524.8 6.3 all_gather.14
  531.0 6.6 conditional.2
  531.0 6.6 fusion
  538.9 8.3 %collective-permute-done = bf16[32,1024]{1,0:T(8,128)(2,1)S(1)} collective-permute-done((bf16[32,1024]{1,0:T(8,128)(2,1)}, bf16[32,1024]{1,0:T(8,128)(2,1)S(1)}, u32[]{:S(2)}, u32[]{:S(2)}) %collective-permute-start) | collective-permute-done | bytes 65568 | tf_op jit(solution)/shard_map/while/body/eval_jaxpr/ppermute | solution.py:23
  548.1 6.3 all_gather.14
  554.4 6.6 conditional.2
  554.4 6.6 fusion
  562.3 8.3 %collective-permute-done = bf16[32,1024]{1,0:T(8,128)(2,1)S(1)} collective-permute-done((bf16[32,1024]{1,0:T(8,128)(2,1)}, bf16[32,1024]{1,0:T(8,128)(2,1)S(1)}, u32[]{:S(2)}, u32[]{:S(2)}) %collective-permute-start) | collective-permute-done | bytes 65568 | tf_op jit(solution)/shard_map/while/body/eval_jaxpr/ppermute | solution.py:23
  571.6 6.3 all_gather.14
  577.9 6.6 conditional.2
  577.9 6.6 fusion
  585.8 8.3 %collective-permute-done = bf16[32,1024]{1,0:T(8,128)(2,1)S(1)} collective-permute-done((bf16[32,1024]{1,0:T(8,128)(2,1)}, bf16[32,1024]{1,0:T(8,128)(2,1)S(1)}, u32[]{:S(2)}, u32[]{:S(2)}) %collective-permute-start) | collective-permute-done | bytes 65568 | tf_op jit(solution)/shard_map/while/body/eval_jaxpr/ppermute | solution.py:23
  595.0 6.3 all_gather.14
  601.2 6.6 conditional.2
  601.2 6.6 fusion
  608.2 10.8 %all-reduce = (bf16[4,32,64]{2,1,0:T(8,128)(2,1)S(1)}, bf16[128,64]{0,1:T(8,128)(2,1)S(1)}) all-reduce(bf16[4,32,64]{2,1,0:T(8,128)(2,1)S(1)} %bitcast.108, bf16[128,64]{0,1:T(8,128)(2,1)S(1)} %convolution_convert_fusion.1), channel_id=1, replica_groups=mesh['section'=16,'dp'=8,'mp'=4] {'mp'}, use_global_device_ids=true, to_apply=%region_5.6 | all-reduce | flops 16384 | bytes 65536 | tf_op jit(solution)/shard_map/psum | solution.py:102
  619.3 18.4 %all-gather = f32[8,4,1024]{2,1,0:T(4,128)S(1)} all-gather(f32[1,4,1024]{2,1,0:T(4,128)S(1)} %broadcast_in_dim_reshape.3), channel_id=1, replica_groups=mesh['section'=16,'dp'=8,'mp'=4] {'dp'}, dimensions={0}, use_global_device_ids=true | all-gather | bytes 147456 | tf_op jit(solution)/shard_map/all_gather | solution.py:118
  642.5 98.5 %psum.23 = f32[16,8,4]{1,0,2:T(8,128)S(1)} all-reduce(f32[16,8,4]{1,0,2:T(8,128)S(1)} %bitcast.109), channel_id=1, replica_groups=mesh['section'=16,'dp'=8,'mp'=4] {'section','dp','mp'}, use_global_device_ids=true, to_apply=%region_6.7 | all-reduce | flops 512 | bytes 4096 | tf_op jit(solution)/shard_map/psum | solution.py:125
  (108 shorter events, 57.2 us)
Async XLA Ops:
  0.6 31.9 %copy-start = (bf16[1,128,1024]{2,1,0:T(8,128)(2,1)S(1)}, bf16[1,128,1024]{2,1,0:T(8,128)(2,1)}, u32[]{:S(2)}) copy-start(bf16[1,128,1024]{2,1,0:T(8,128)(2,1)} %param.13) | copy-start | bytes 786436
  5.9 11.0 %copy-start.5 = (s32[8,8]{1,0:T(8,128)S(1)}, s32[8,8]{1,0:T(8,128)}, u32[]{:S(2)}) copy-start(s32[8,8]{1,0:T(8,128)} %param.19) | copy-start | bytes 772
  5.9 26.7 %copy-start.2 = (bf16[1,1024,64]{1,2,0:T(8,128)(2,1)S(1)}, bf16[1,1024,64]{1,2,0:T(8,128)(2,1)}, u32[]{:S(2)}) copy-start(bf16[1,1024,64]{1,2,0:T(8,128)(2,1)} %param.16) | copy-start | bytes 393220
  5.9 197.9 %all-to-all-start = ((bf16[8,1024,512]{2,1,0:T(8,128)(2,1)}), bf16[8,1024,512]{2,1,0:T(8,128)(2,1)}, u32[]{:S(2)}, u32[]{:S(2)}) async-start(bf16[8,1024,512]{2,1,0:T(8,128)(2,1)} %stack.3), calls=%async_computation | async-start | bytes 16777216 | tf_op jit(solution)/shard_map/all_to_all | solution.py:13
  227.1 380.7 %copy-start.3 = (bf16[1,1024,64]{1,2,0:T(8,128)(2,1)S(1)}, bf16[1,1024,64]{1,2,0:T(8,128)(2,1)}, u32[]{:S(2)}) copy-start(bf16[1,1024,64]{1,2,0:T(8,128)(2,1)} %param.17) | copy-start | bytes 393220
  227.1 410.6 %copy-start.1 = (f32[1,2,1024]{2,1,0:T(2,128)S(1)}, f32[1,2,1024]{2,1,0:T(2,128)}, u32[]{:S(2)}) copy-start(f32[1,2,1024]{2,1,0:T(2,128)} %param.18) | copy-start | bytes 24580
  227.1 5.3 collective-permute-start
  241.3 5.6 collective-permute-start
  255.1 5.6 collective-permute-start
  268.9 6.6 collective-permute-start
  283.5 7.1 collective-permute-start
  298.5 7.1 collective-permute-start
  313.5 7.1 collective-permute-start
  328.5 7.1 collective-permute-start
  343.6 7.1 collective-permute-start
  358.6 7.3 collective-permute-start
  373.8 9.5 %collective-permute-start = (bf16[32,1024]{1,0:T(8,128)(2,1)}, bf16[32,1024]{1,0:T(8,128)(2,1)S(1)}, u32[]{:S(2)}, u32[]{:S(2)}) collective-permute-start(bf16[32,1024]{1,0:T(8,128)(2,1)} %get-tuple-element.309), channel_id=1, source_target_pairs={{32,0},{64,32},{96,64},{128,96},{160,128},{192,160},{224,192},{256... | collective-permute-start | bytes 196616 | tf_op jit(solution)/shard_map/while/body/eval_jaxpr/ppermute | solution.py:23
  391.3 9.5 %collective-permute-start = (bf16[32,1024]{1,0:T(8,128)(2,1)}, bf16[32,1024]{1,0:T(8,128)(2,1)S(1)}, u32[]{:S(2)}, u32[]{:S(2)}) collective-permute-start(bf16[32,1024]{1,0:T(8,128)(2,1)} %get-tuple-element.309), channel_id=1, source_target_pairs={{32,0},{64,32},{96,64},{128,96},{160,128},{192,160},{224,192},{256... | collective-permute-start | bytes 196616 | tf_op jit(solution)/shard_map/while/body/eval_jaxpr/ppermute | solution.py:23
  408.7 9.5 %collective-permute-start = (bf16[32,1024]{1,0:T(8,128)(2,1)}, bf16[32,1024]{1,0:T(8,128)(2,1)S(1)}, u32[]{:S(2)}, u32[]{:S(2)}) collective-permute-start(bf16[32,1024]{1,0:T(8,128)(2,1)} %get-tuple-element.309), channel_id=1, source_target_pairs={{32,0},{64,32},{96,64},{128,96},{160,128},{192,160},{224,192},{256... | collective-permute-start | bytes 196616 | tf_op jit(solution)/shard_map/while/body/eval_jaxpr/ppermute | solution.py:23
  426.1 9.5 %collective-permute-start = (bf16[32,1024]{1,0:T(8,128)(2,1)}, bf16[32,1024]{1,0:T(8,128)(2,1)S(1)}, u32[]{:S(2)}, u32[]{:S(2)}) collective-permute-start(bf16[32,1024]{1,0:T(8,128)(2,1)} %get-tuple-element.309), channel_id=1, source_target_pairs={{32,0},{64,32},{96,64},{128,96},{160,128},{192,160},{224,192},{256... | collective-permute-start | bytes 196616 | tf_op jit(solution)/shard_map/while/body/eval_jaxpr/ppermute | solution.py:23
  443.5 9.5 %collective-permute-start = (bf16[32,1024]{1,0:T(8,128)(2,1)}, bf16[32,1024]{1,0:T(8,128)(2,1)S(1)}, u32[]{:S(2)}, u32[]{:S(2)}) collective-permute-start(bf16[32,1024]{1,0:T(8,128)(2,1)} %get-tuple-element.309), channel_id=1, source_target_pairs={{32,0},{64,32},{96,64},{128,96},{160,128},{192,160},{224,192},{256... | collective-permute-start | bytes 196616 | tf_op jit(solution)/shard_map/while/body/eval_jaxpr/ppermute | solution.py:23
  460.9 62.9 %collective-permute-start = (bf16[32,1024]{1,0:T(8,128)(2,1)}, bf16[32,1024]{1,0:T(8,128)(2,1)S(1)}, u32[]{:S(2)}, u32[]{:S(2)}) collective-permute-start(bf16[32,1024]{1,0:T(8,128)(2,1)} %get-tuple-element.309), channel_id=1, source_target_pairs={{32,0},{64,32},{96,64},{128,96},{160,128},{192,160},{224,192},{256... | collective-permute-start | bytes 196616 | tf_op jit(solution)/shard_map/while/body/eval_jaxpr/ppermute | solution.py:23
  537.6 9.6 %collective-permute-start = (bf16[32,1024]{1,0:T(8,128)(2,1)}, bf16[32,1024]{1,0:T(8,128)(2,1)S(1)}, u32[]{:S(2)}, u32[]{:S(2)}) collective-permute-start(bf16[32,1024]{1,0:T(8,128)(2,1)} %get-tuple-element.309), channel_id=1, source_target_pairs={{32,0},{64,32},{96,64},{128,96},{160,128},{192,160},{224,192},{256... | collective-permute-start | bytes 196616 | tf_op jit(solution)/shard_map/while/body/eval_jaxpr/ppermute | solution.py:23
  561.0 9.6 %collective-permute-start = (bf16[32,1024]{1,0:T(8,128)(2,1)}, bf16[32,1024]{1,0:T(8,128)(2,1)S(1)}, u32[]{:S(2)}, u32[]{:S(2)}) collective-permute-start(bf16[32,1024]{1,0:T(8,128)(2,1)} %get-tuple-element.309), channel_id=1, source_target_pairs={{32,0},{64,32},{96,64},{128,96},{160,128},{192,160},{224,192},{256... | collective-permute-start | bytes 196616 | tf_op jit(solution)/shard_map/while/body/eval_jaxpr/ppermute | solution.py:23
  584.4 9.6 %collective-permute-start = (bf16[32,1024]{1,0:T(8,128)(2,1)}, bf16[32,1024]{1,0:T(8,128)(2,1)S(1)}, u32[]{:S(2)}, u32[]{:S(2)}) collective-permute-start(bf16[32,1024]{1,0:T(8,128)(2,1)} %get-tuple-element.309), channel_id=1, source_target_pairs={{32,0},{64,32},{96,64},{128,96},{160,128},{192,160},{224,192},{256... | collective-permute-start | bytes 196616 | tf_op jit(solution)/shard_map/while/body/eval_jaxpr/ppermute | solution.py:23
  619.3 122.4 %copy-start.4 = (f32[1,4,1024]{2,1,0:T(4,128)}, f32[1,4,1024]{2,1,0:T(4,128)S(1)}, u32[]{:S(2)}) copy-start(f32[1,4,1024]{2,1,0:T(4,128)S(1)} %broadcast_in_dim_reshape.3) | copy-start | bytes 49156
